TPU v7x, 256 devices: a whole 4x4x8 slice. The times are simulated.
256 devices in a mesh: shot: 16 (over y, x_lo, core), space: 16 (over z, x_hi).
Axes of the slice: x: 4 (x_hi: 2, x_lo: 2; x = x_hi * 2 + x_lo), y: 4, z: 8, core: 2. Of those that a mesh axis runs over, the one named last changes fastest.
Arguments:
- courant: float32 [128, 128, 128], P('space'), may hold values from 0.03 to 0.18
- checkpoint: float32 [16, 2, 2048, 8, 128], P('shot', None, 'space'), may hold values from -6 to 6
- block_target: int32 [16, 2048], P('shot'), may hold values from 0 to 2047, as said below
- adjoint_state: float32 [16, 2, 128, 128, 128], P('shot', None, 'space'), may hold values from -6 to 6
- wavelet: float32 [16, 4], P('shot'), may hold values from -8 to 8
- source_cell: int32 [16], P('shot'), may hold values from 0 to 2097151
- receiver_cell: int32 [16, 512], P('shot'), may hold values from 0 to 2097151
- residual: float32 [16, 4, 512], P('shot'), may hold values from -6 to 6
- check_rows: int32 [16, 128, 16], P('space'), may hold values from 0 to 1023
Outputs:
- gradient: float32 [128, 128, 128], P('space', 'shot')
- adjoint_carry: float32 [16, 2, 128, 128, 128], P('shot', None, 'space')
- checksums: float32 [16, 128, 128], P('space', 'shot')
Inputs may be any that keep to these rules, and one draw needn't show every extreme that they name: `block_target`: each shot's row is a permutation of the block positions. The stored blocks of one device (aligned blocks of 128 entries) name at most 32 positions of any one slab (128 consecutive positions); each device names exactly 32 of one slab, and each slab is named exactly 32 times by one device.
All inputs are finite; a program needn't handle non-finite values.
Results may differ from a plain program's by a relative error of at most 0.0003.
Values sent between devices are 32-bit elements; how exact they have to be, the bound alone decides.
No kernel may reach another device: no remote copies, remote signals or barrier semaphores. Data moves between devices by JAX's collectives and lax.ppermute only.
A program may use at most 128 MiB of HBM per device.

v0:
```python
import jax
import jax.numpy as jnp
from jax import lax
from jax.sharding import PartitionSpec as P

STENCIL = (-205.0 / 72.0, 8.0 / 5.0, -1.0 / 5.0, 8.0 / 315.0, -1.0 / 560.0)


def padded_2(array, sides, width):
    for axis, dim in sides:
        devices, length = (lax.axis_size(axis), array.shape[dim])
        up = [(i, (i + 1) % devices) for i in range(devices - 1)]
        down = [(j, i) for i, j in up]
        last = lax.slice_in_dim(array, length - width, length, axis=dim)
        initial = lax.slice_in_dim(array, 0, width, axis=dim)
        before = lax.ppermute(last, axis, up)
        after = lax.ppermute(initial, axis, down)
        array = jnp.concatenate([before, array, after], axis=dim)
    return array


def laplace(field):
    length = field.shape[0] - 8
    height = field.shape[1]
    breadth = field.shape[2]
    padded = jnp.pad(field, ((0, 0), (4, 4), (4, 4)))
    summed = 3.0 * STENCIL[0] * padded[4 : 4 + length, 4 : 4 + height, 4 : 4 + breadth]
    for offset in range(1, 5):
        summed = summed + STENCIL[offset] * (
            padded[4 + offset : 4 + offset + length, 4 : 4 + height, 4 : 4 + breadth]
            + padded[4 - offset : 4 - offset + length, 4 : 4 + height, 4 : 4 + breadth]
        )
    for offset in range(1, 5):
        summed = summed + STENCIL[offset] * (
            padded[4 : 4 + length, 4 + offset : 4 + offset + height, 4 : 4 + breadth]
            + padded[4 : 4 + length, 4 - offset : 4 - offset + height, 4 : 4 + breadth]
        )
    for offset in range(1, 5):
        summed = summed + STENCIL[offset] * (
            padded[4 : 4 + length, 4 : 4 + height, 4 + offset : 4 + offset + breadth]
            + padded[4 : 4 + length, 4 : 4 + height, 4 - offset : 4 - offset + breadth]
        )
    return summed


def inject(field, cell_index, values, first_row):
    plane_cells = field.shape[1] * field.shape[2]
    local_cell = cell_index - first_row * plane_cells
    inside = (local_cell >= 0) & (local_cell < field.shape[0] * plane_cells)
    target = jnp.where(inside, local_cell, field.shape[0] * plane_cells)
    flattened = field.reshape(-1).at[target].add(values, mode="drop")
    return flattened.reshape(field.shape)


def advance(before, current_ext, courant, wave_value, source, first_row):
    following = 2.0 * current_ext[4:-4] - before + courant * laplace(current_ext)
    return inject(following, source, wave_value, first_row)


def retreat(following, current, weighted_ext, values, cell_index, first_row):
    earlier = 2.0 * current - following + laplace(weighted_ext)
    return inject(earlier, cell_index, values, first_row)


def extend(field):
    return padded_2(field, (("space", 0),), 4)


def body(
    courant,
    checkpoint,
    block_target,
    adjoint_state,
    wavelet,
    source_cell,
    receiver_cell,
    residual,
    check_rows,
):
    devices = lax.axis_size("space")
    position = lax.axis_index("space")
    length, height, breadth = courant.shape
    first_row = position * length
    per_device = checkpoint.shape[2]
    block_rows = checkpoint.shape[3]
    capacity = per_device // 4
    targets = block_target[0]
    payload = checkpoint[0]
    peers = targets // per_device
    matches = (peers[:, None] == jnp.arange(devices, dtype=jnp.int32)[None, :]).astype(jnp.int32)
    grouped = matches.reshape(devices, per_device, devices)
    ranking = jnp.sum((jnp.cumsum(grouped, axis=1) - grouped) * grouped, axis=2)
    peer_grid = peers.reshape(devices, per_device)
    own_peers = lax.dynamic_index_in_dim(peer_grid, position, 0, keepdims=False)
    own_ranks = lax.dynamic_index_in_dim(ranking, position, 0, keepdims=False)
    slot_of = own_peers * capacity + own_ranks
    outgoing = (
        jnp.zeros((2, devices * capacity, block_rows, breadth), jnp.float32)
        .at[:, slot_of]
        .set(payload)
    )
    outgoing = outgoing.reshape(2, devices, capacity, block_rows, breadth)
    incoming = lax.all_to_all(outgoing, "space", split_axis=1, concat_axis=1, tiled=True)
    incoming = incoming.reshape(2, devices * capacity, block_rows, breadth)
    sender_grid = jnp.arange(devices, dtype=jnp.int32)[:, None] * capacity + ranking
    owned = peer_grid == position
    local_block = (targets % per_device).reshape(devices, per_device)
    where_from = (
        jnp.zeros((per_device,), jnp.int32)
        .at[jnp.where(owned, local_block, per_device).reshape(-1)]
        .set(sender_grid.reshape(-1), mode="drop")
    )
    placed = jnp.take(incoming, where_from, axis=1)
    levels = placed.reshape(2, length, height, breadth)
    wavelet_row = wavelet[0]
    receivers = receiver_cell[0]
    traces = residual[0]
    horizon = wavelet_row.shape[0]
    fields = [levels[0], levels[1]]
    adjoints = [None] * (horizon + 2)
    adjoints[horizon + 1] = adjoint_state[0, 0]
    adjoints[horizon] = adjoint_state[0, 1]
    for moment in range(1, horizon + 1):
        fields.append(
            advance(
                fields[-2],
                extend(fields[-1]),
                courant,
                wavelet_row[moment - 1 : moment],
                source_cell,
                first_row,
            )
        )
    for moment in range(horizon, 0, -1):
        weighted = extend(courant * adjoints[moment])
        adjoints[moment - 1] = retreat(
            adjoints[moment + 1],
            adjoints[moment],
            weighted,
            traces[moment - 1],
            receivers,
            first_row,
        )
    partial_value = jnp.zeros((length, height, breadth), jnp.float32)
    for moment in range(1, horizon + 1):
        partial_value = partial_value + adjoints[moment] * (
            fields[moment + 1] - 2.0 * fields[moment] + fields[moment - 1]
        )
    slab_rows = partial_value.reshape(length * height, breadth)
    check_part = jnp.sum(slab_rows[check_rows[0]], axis=1)
    grad_share = lax.psum_scatter(partial_value, "shot", scatter_dimension=1, tiled=True)
    check_share = lax.psum_scatter(check_part, "shot", scatter_dimension=0, tiled=True)
    adjoint_carry = jnp.stack([adjoints[1], adjoints[0]])[None]
    return (grad_share, adjoint_carry, check_share[None])


def solution(mesh):
    in_specs = (
        P("space", None, None),
        P("shot", None, "space", None, None),
        P("shot", None),
        P("shot", None, "space", None, None),
        P("shot", None),
        P("shot"),
        P("shot", None),
        P("shot", None, None),
        P("space", None, None),
    )
    out_specs = (
        P("space", "shot", None),
        P("shot", None, "space", None, None),
        P("space", "shot", None),
    )
    return jax.shard_map(body, mesh=mesh, in_specs=in_specs, out_specs=out_specs, check_vma=False)
```

profile of v0, /device:TPU:4, one launch (start us, length us, event | category | flops | bytes accessed | tf_op | source)
XLA Modules:
  0.0 528.2 jit_solution(15008843376083713308)
XLA Ops:
  14.6 13.6 %scatter_fusion.3 = f32[2,512,8,128]{3,2,1,0:T(8,128)} fusion(f32[2,512,8,128]{3,2,1,0:T(8,128)} %broadcast_in_dim.48, s32[128]{0:T(128)S(1)} %fusion.310, f32[128,2,8,128]{3,2,1,0:T(8,128)S(1)} %copy.34), kind=kCustom, calls=%fused_computation.6 | custom fusion | bytes 3146240 | tf_op jit(solution)/shard_map/scatter | solution.py:100
  28.2 4.7 copy.35
  32.9 11.6 %all-to-all-start = ((f32[2,16,32,8,128]{4,3,2,0,1:T(8,128)}), f32[2,16,32,8,128]{4,3,2,0,1:T(8,128)}, u32[]{:S(2)}, u32[]{:S(2)}) async-start(f32[2,16,32,8,128]{4,3,2,0,1:T(8,128)} %copy.35), calls=%async_computation | async-start | bytes 8388608 | tf_op jit(solution)/shard_map/all_to_all | solution.py:103
  46.7 6.2 %collective-permute-start.1 = (f32[4,128,128]{2,1,0:T(8,128)S(1)}, f32[4,128,128]{2,1,0:T(8,128)S(1)}, u32[]{:S(2)}, u32[]{:S(2)}) collective-permute-start(f32[4,128,128]{2,1,0:T(8,128)S(1)} %get-tuple-element.64), channel_id=1, source_target_pairs={{0,1},{1,2},{2,3},{3,4},{4,5},{5,6},{6,7},{7,8},{8,9},{9,10},{10,1... | collective-permute-start | bytes 786440 | tf_op jit(solution)/shard_map/ppermute | solution.py:16
  53.2 8.0 %scatter_custom_fusion.3 = s32[128]{0:T(128)S(1)} fusion(s32[2048]{0:T(1024)S(1)} %bitcast.210, s32[2048]{0:T(1024)S(1)} %add_bitcast_fusion, s32[]{:T(128)} %constant.152.clone.1), kind=kCustom, calls=%fused_computation.564 | custom fusion | bytes 516 | tf_op jit(solution)/shard_map/scatter | solution.py:111
  63.5 82.6 %collective-permute-done = f32[4,128,128]{2,1,0:T(8,128)S(1)} collective-permute-done((f32[4,128,128]{2,1,0:T(8,128)S(1)}, f32[4,128,128]{2,1,0:T(8,128)S(1)}, u32[]{:S(2)}, u32[]{:S(2)}) %collective-permute-start) | collective-permute-done | bytes 262176 | tf_op jit(solution)/shard_map/ppermute | solution.py:17
  148.6 3.5 fusion.199
  152.1 3.7 scatter_fusion
  158.0 6.3 %collective-permute-start.3 = (f32[4,128,128]{2,1,0:T(8,128)S(1)}, f32[4,128,128]{2,1,0:T(8,128)}, u32[]{:S(2)}, u32[]{:S(2)}) collective-permute-start(f32[4,128,128]{2,1,0:T(8,128)S(1)} %get-tuple-element.62), channel_id=1, source_target_pairs={{0,1},{1,2},{2,3},{3,4},{4,5},{5,6},{6,7},{7,8},{8,9},{9,10},{10,1... | collective-permute-start | bytes 786440 | tf_op jit(solution)/shard_map/ppermute | solution.py:16
  167.7 5.6 %collective-permute-done.3 = f32[4,128,128]{2,1,0:T(8,128)} collective-permute-done((f32[4,128,128]{2,1,0:T(8,128)S(1)}, f32[4,128,128]{2,1,0:T(8,128)}, u32[]{:S(2)}, u32[]{:S(2)}) %collective-permute-start.3) | collective-permute-done | bytes 262176 | tf_op jit(solution)/shard_map/ppermute | solution.py:16
  175.1 4.7 copy.36
  179.8 4.0 gather_fusion
  187.2 6.6 %collective-permute-start.7 = (f32[4,128,128]{2,1,0:T(8,128)S(1)}, f32[4,128,128]{2,1,0:T(8,128)S(1)}, u32[]{:S(2)}, u32[]{:S(2)}) collective-permute-start(f32[4,128,128]{2,1,0:T(8,128)S(1)} %bitcast.199), channel_id=1, source_target_pairs={{0,1},{1,2},{2,3},{3,4},{4,5},{5,6},{6,7},{7,8},{8,9},{9,10},{10,1... | collective-permute-start | bytes 786440 | tf_op jit(solution)/shard_map/ppermute | solution.py:16
  197.9 5.5 %collective-permute-done.7 = f32[4,128,128]{2,1,0:T(8,128)S(1)} collective-permute-done((f32[4,128,128]{2,1,0:T(8,128)S(1)}, f32[4,128,128]{2,1,0:T(8,128)S(1)}, u32[]{:S(2)}, u32[]{:S(2)}) %collective-permute-start.7) | collective-permute-done | bytes 262176 | tf_op jit(solution)/shard_map/ppermute | solution.py:16
  205.4 11.8 %fusion.124 = f32[8,128,128]{2,1,0:T(8,128)S(1)} fusion(f32[8,128,128]{2,1,0:T(8,128)S(1)} %copy-done.3, f32[8,128,128]{2,1,0:T(8,128)S(1)} %bitcast.188, f32[4,128,128]{2,1,0:T(8,128)} %copy-done.31, f32[4,128,128]{2,1,0:T(8,128)} %copy-done.30, f32[16,136,136]{2,1,0:T(8,128)} %select_maximum_fusion.8, f32[8,128,128]{2,1,0:T(8,128)} %bitcast.194), kind=kLoop, calls=%fused_computation.252 | loop fusion | flops 6422528 | bytes 11010048 | tf_op jit(solution)/shard_map/add | solution.py:56
  222.1 6.3 %collective-permute-start.9 = (f32[4,128,128]{2,1,0:T(8,128)}, f32[4,128,128]{2,1,0:T(8,128)}, u32[]{:S(2)}, u32[]{:S(2)}) collective-permute-start(f32[4,128,128]{2,1,0:T(8,128)} %bitcast.33), channel_id=1, source_target_pairs={{0,1},{1,2},{2,3},{3,4},{4,5},{5,6},{6,7},{7,8},{8,9},{9,10},{10,1... | collective-permute-start | bytes 786440 | tf_op jit(solution)/shard_map/ppermute | solution.py:16
  231.9 3.8 scatter_fusion.1
  238.6 6.3 %collective-permute-start.5 = (f32[4,128,128]{2,1,0:T(8,128)}, f32[4,128,128]{2,1,0:T(8,128)}, u32[]{:S(2)}, u32[]{:S(2)}) collective-permute-start(f32[4,128,128]{2,1,0:T(8,128)} %get-tuple-element.60), channel_id=1, source_target_pairs={{0,1},{1,2},{2,3},{3,4},{4,5},{5,6},{6,7},{7,8},{8,9},{9,10},{10,1... | collective-permute-start | bytes 786440 | tf_op jit(solution)/shard_map/ppermute | solution.py:16
  246.7 3.5 fusion.98
  254.3 6.5 %collective-permute-start.11 = (f32[4,128,128]{2,1,0:T(8,128)S(1)}, f32[4,128,128]{2,1,0:T(8,128)S(1)}, u32[]{:S(2)}, u32[]{:S(2)}) collective-permute-start(f32[4,128,128]{2,1,0:T(8,128)S(1)} %bitcast.197), channel_id=1, source_target_pairs={{0,1},{1,2},{2,3},{3,4},{4,5},{5,6},{6,7},{7,8},{8,9},{9,10},{10,1... | collective-permute-start | bytes 786440 | tf_op jit(solution)/shard_map/ppermute | solution.py:16
  263.9 5.5 %collective-permute-done.11 = f32[4,128,128]{2,1,0:T(8,128)S(1)} collective-permute-done((f32[4,128,128]{2,1,0:T(8,128)S(1)}, f32[4,128,128]{2,1,0:T(8,128)S(1)}, u32[]{:S(2)}, u32[]{:S(2)}) %collective-permute-start.11) | collective-permute-done | bytes 262176 | tf_op jit(solution)/shard_map/ppermute | solution.py:16
  272.1 12.4 %fusion.72 = f32[8,128,128]{2,1,0:T(8,128)} fusion(f32[8,128,128]{2,1,0:T(8,128)S(1)} %copy-done.5, f32[8,128,128]{2,1,0:T(8,128)S(1)} %bitcast.177, f32[4,128,128]{2,1,0:T(8,128)} %copy-done.29, f32[4,128,128]{2,1,0:T(8,128)} %copy-done.28, f32[16,136,136]{2,1,0:T(8,128)} %select_maximum_fusion.4, f32[8,128,128]{2,1,0:T(8,128)S(1)} %bitcast.173), kind=kLoop, calls=%fused_computation.200 | loop fusion | flops 6422528 | bytes 11010048 | tf_op jit(solution)/shard_map/add | solution.py:56
  291.7 6.3 %collective-permute-start.13 = (f32[4,128,128]{2,1,0:T(8,128)}, f32[4,128,128]{2,1,0:T(8,128)}, u32[]{:S(2)}, u32[]{:S(2)}) collective-permute-start(f32[4,128,128]{2,1,0:T(8,128)} %bitcast.43), channel_id=1, source_target_pairs={{0,1},{1,2},{2,3},{3,4},{4,5},{5,6},{6,7},{7,8},{8,9},{9,10},{10,1... | collective-permute-start | bytes 786440 | tf_op jit(solution)/shard_map/ppermute | solution.py:16
  298.0 4.8 fusion.149
  302.8 5.0 scatter_fusion.2
  310.1 5.1 fusion.46
  325.5 6.3 %collective-permute-start.15 = (f32[4,128,128]{2,1,0:T(8,128)S(1)}, f32[4,128,128]{2,1,0:T(8,128)}, u32[]{:S(2)}, u32[]{:S(2)}) collective-permute-start(f32[4,128,128]{2,1,0:T(8,128)S(1)} %get-tuple-element.56), channel_id=1, source_target_pairs={{0,1},{1,2},{2,3},{3,4},{4,5},{5,6},{6,7},{7,8},{8,9},{9,10},{10,1... | collective-permute-start | bytes 786440 | tf_op jit(solution)/shard_map/ppermute | solution.py:16
  331.9 5.5 %gather_fusion.1 = f32[2048,128]{1,0:T(8,128)S(1)} fusion(f32[1024,128]{1,0:T(8,128)S(1)} %fusion.293, s32[2048]{0:T(1024)S(1)} %broadcast_clamp_fusion), kind=kCustom, calls=%fused_computation.1 | custom fusion | bytes 2105344 | tf_op jit(solution)/shard_map/gather | solution.py:150
  339.8 115.9 %all-reduce.11.cloned.1.call-done = f32[128,128]{1,0:T(8,128)} async-done(((f32[128,128]{1,0:T(8,128)}), f32[128,128]{1,0:T(8,128)}) %all-reduce.11.cloned.1.call-update) | async-done | bytes 65552
  458.7 4.9 fusion.20
  463.6 4.9 scatter_fusion.4
  470.5 50.8 %reduce-scatter.2.cloned.1.call-done = f32[8,8,128]{2,1,0:T(8,128)} async-done(((f32[8,128,128]{2,1,0:T(8,128)}), f32[8,8,128]{2,1,0:T(8,128)}) %reduce-scatter.2.cloned.1.call-update) | async-done | bytes 32784 | tf_op jit(solution)/shard_map/reduce_scatter | solution.py:151
  (159 shorter events, 79.2 us)
Async XLA Ops:
  32.9 142.2 %all-to-all-start = ((f32[2,16,32,8,128]{4,3,2,0,1:T(8,128)}), f32[2,16,32,8,128]{4,3,2,0,1:T(8,128)}, u32[]{:S(2)}, u32[]{:S(2)}) async-start(f32[2,16,32,8,128]{4,3,2,0,1:T(8,128)} %copy.35), calls=%async_computation | async-start | bytes 8388608 | tf_op jit(solution)/shard_map/all_to_all | solution.py:103
  44.4 17.8 %copy-start.36 = (s32[1,512]{1,0:T(1,128)S(1)}, s32[1,512]{1,0:T(1,128)}, u32[]{:S(2)}) copy-start(s32[1,512]{1,0:T(1,128)} %param.23) | copy-start | bytes 6148
  44.4 17.8 %copy-start.33 = (f32[1,4,512]{2,1,0:T(4,128)S(1)}, f32[1,4,512]{2,1,0:T(4,128)}, u32[]{:S(2)}) copy-start(f32[1,4,512]{2,1,0:T(4,128)} %param.24) | copy-start | bytes 24580
  44.5 18.4 %copy-start.35 = (f32[1,4]{1,0:T(1,128)S(1)}, f32[1,4]{1,0:T(1,128)}, u32[]{:S(2)}) copy-start(f32[1,4]{1,0:T(1,128)} %param.21) | copy-start | bytes 52
  44.5 19.0 %copy-start.34 = (s32[1,128,16]{1,2,0:T(8,128)S(1)}, s32[1,128,16]{1,2,0:T(8,128)}, u32[]{:S(2)}) copy-start(s32[1,128,16]{1,2,0:T(8,128)} %param.25) | copy-start | bytes 24580
  44.5 411.2 %all-reduce.11.cloned.1.call-start = ((), (), s32[]{:S(2)}) async-start(), calls=%async_computation.3 | async-start | bytes 131072
  44.6 101.4 %copy-start.22 = (f32[8,128,128]{2,1,0:T(8,128)}, f32[8,128,128]{2,1,0:T(8,128)S(1)}, u32[]{:S(2)}) copy-start(f32[8,128,128]{2,1,0:T(8,128)S(1)} %bitcast_multiply_fusion.5) | copy-start | bytes 1572868
  44.7 101.4 %collective-permute-start = (f32[4,128,128]{2,1,0:T(8,128)S(1)}, f32[4,128,128]{2,1,0:T(8,128)S(1)}, u32[]{:S(2)}, u32[]{:S(2)}) collective-permute-start(f32[4,128,128]{2,1,0:T(8,128)S(1)} %get-tuple-element.63), channel_id=1, source_target_pairs={{1,0},{2,1},{3,2},{4,3},{5,4},{6,5},{7,6},{8,7},{9,8},{10,9},{11,1... | collective-permute-start | bytes 786440 | tf_op jit(solution)/shard_map/ppermute | solution.py:17
  46.7 99.3 %collective-permute-start.1 = (f32[4,128,128]{2,1,0:T(8,128)S(1)}, f32[4,128,128]{2,1,0:T(8,128)S(1)}, u32[]{:S(2)}, u32[]{:S(2)}) collective-permute-start(f32[4,128,128]{2,1,0:T(8,128)S(1)} %get-tuple-element.64), channel_id=1, source_target_pairs={{0,1},{1,2},{2,3},{3,4},{4,5},{5,6},{6,7},{7,8},{8,9},{9,10},{10,1... | collective-permute-start | bytes 786440 | tf_op jit(solution)/shard_map/ppermute | solution.py:16
  155.9 11.9 %copy-start.19 = (f32[8,128,128]{2,1,0:T(8,128)}, f32[8,128,128]{2,1,0:T(8,128)S(1)}, u32[]{:S(2)}) copy-start(f32[8,128,128]{2,1,0:T(8,128)S(1)} %mul.453) | copy-start | bytes 1572868
  155.9 11.8 %collective-permute-start.2 = (f32[4,128,128]{2,1,0:T(8,128)S(1)}, f32[4,128,128]{2,1,0:T(8,128)S(1)}, u32[]{:S(2)}, u32[]{:S(2)}) collective-permute-start(f32[4,128,128]{2,1,0:T(8,128)S(1)} %get-tuple-element.61), channel_id=1, source_target_pairs={{1,0},{2,1},{3,2},{4,3},{5,4},{6,5},{7,6},{8,7},{9,8},{10,9},{11,1... | collective-permute-start | bytes 786440 | tf_op jit(solution)/shard_map/ppermute | solution.py:17
  158.0 15.4 %collective-permute-start.3 = (f32[4,128,128]{2,1,0:T(8,128)S(1)}, f32[4,128,128]{2,1,0:T(8,128)}, u32[]{:S(2)}, u32[]{:S(2)}) collective-permute-start(f32[4,128,128]{2,1,0:T(8,128)S(1)} %get-tuple-element.62), channel_id=1, source_target_pairs={{0,1},{1,2},{2,3},{3,4},{4,5},{5,6},{6,7},{7,8},{8,9},{9,10},{10,1... | collective-permute-start | bytes 786440 | tf_op jit(solution)/shard_map/ppermute | solution.py:16
  185.2 12.6 %collective-permute-start.6 = (f32[4,128,128]{2,1,0:T(8,128)S(1)}, f32[4,128,128]{2,1,0:T(8,128)S(1)}, u32[]{:S(2)}, u32[]{:S(2)}) collective-permute-start(f32[4,128,128]{2,1,0:T(8,128)S(1)} %bitcast.200), channel_id=1, source_target_pairs={{1,0},{2,1},{3,2},{4,3},{5,4},{6,5},{7,6},{8,7},{9,8},{10,9},{11,1... | collective-permute-start | bytes 786440 | tf_op jit(solution)/shard_map/ppermute | solution.py:17
  187.2 18.3 %copy-start.3 = (f32[8,128,128]{2,1,0:T(8,128)S(1)}, f32[8,128,128]{2,1,0:T(8,128)}, u32[]{:S(2)}) copy-start(f32[8,128,128]{2,1,0:T(8,128)} %param.17) | copy-start | bytes 1572868
  187.2 16.2 %collective-permute-start.7 = (f32[4,128,128]{2,1,0:T(8,128)S(1)}, f32[4,128,128]{2,1,0:T(8,128)S(1)}, u32[]{:S(2)}, u32[]{:S(2)}) collective-permute-start(f32[4,128,128]{2,1,0:T(8,128)S(1)} %bitcast.199), channel_id=1, source_target_pairs={{0,1},{1,2},{2,3},{3,4},{4,5},{5,6},{6,7},{7,8},{8,9},{9,10},{10,1... | collective-permute-start | bytes 786440 | tf_op jit(solution)/shard_map/ppermute | solution.py:16
  194.7 22.5 %copy-start.13 = (f32[1,128,8,128]{3,2,0,1:T(8,128)}, f32[1,128,8,128]{3,2,0,1:T(8,128)S(1)}, u32[]{:S(2)}) copy-start(f32[1,128,8,128]{3,2,0,1:T(8,128)S(1)} %get-tuple-element.52) | copy-start | bytes 1572868
  205.4 23.0 %copy-start.20 = (f32[8,128,128]{2,1,0:T(8,128)S(1)}, f32[8,128,128]{2,1,0:T(8,128)}, u32[]{:S(2)}) copy-start(f32[8,128,128]{2,1,0:T(8,128)} %copy-done.19) | copy-start | bytes 1572868
  219.3 12.6 %copy-start.7 = (f32[131072]{0:T(1024)}, f32[131072]{0:T(1024)S(1)}, u32[]{:S(2)}) copy-start(f32[131072]{0:T(1024)S(1)} %fusion.306) | copy-start | bytes 1572868
  220.2 24.7 %collective-permute-start.8 = (f32[4,128,128]{2,1,0:T(8,128)}, f32[4,128,128]{2,1,0:T(8,128)}, u32[]{:S(2)}, u32[]{:S(2)}) collective-permute-start(f32[4,128,128]{2,1,0:T(8,128)} %bitcast.32), channel_id=1, source_target_pairs={{1,0},{2,1},{3,2},{4,3},{5,4},{6,5},{7,6},{8,7},{9,8},{10,9},{11,1... | collective-permute-start | bytes 786440 | tf_op jit(solution)/shard_map/ppermute | solution.py:17
  222.1 22.8 %collective-permute-start.9 = (f32[4,128,128]{2,1,0:T(8,128)}, f32[4,128,128]{2,1,0:T(8,128)}, u32[]{:S(2)}, u32[]{:S(2)}) collective-permute-start(f32[4,128,128]{2,1,0:T(8,128)} %bitcast.33), channel_id=1, source_target_pairs={{0,1},{1,2},{2,3},{3,4},{4,5},{5,6},{6,7},{7,8},{8,9},{9,10},{10,1... | collective-permute-start | bytes 786440 | tf_op jit(solution)/shard_map/ppermute | solution.py:16
  236.7 24.2 %collective-permute-start.4 = (f32[4,128,128]{2,1,0:T(8,128)}, f32[4,128,128]{2,1,0:T(8,128)S(1)}, u32[]{:S(2)}, u32[]{:S(2)}) collective-permute-start(f32[4,128,128]{2,1,0:T(8,128)} %get-tuple-element.59), channel_id=1, source_target_pairs={{1,0},{2,1},{3,2},{4,3},{5,4},{6,5},{7,6},{8,7},{9,8},{10,9},{11,1... | collective-permute-start | bytes 786440 | tf_op jit(solution)/shard_map/ppermute | solution.py:17
  238.6 22.3 %collective-permute-start.5 = (f32[4,128,128]{2,1,0:T(8,128)}, f32[4,128,128]{2,1,0:T(8,128)}, u32[]{:S(2)}, u32[]{:S(2)}) collective-permute-start(f32[4,128,128]{2,1,0:T(8,128)} %get-tuple-element.60), channel_id=1, source_target_pairs={{0,1},{1,2},{2,3},{3,4},{4,5},{5,6},{6,7},{7,8},{8,9},{9,10},{10,1... | collective-permute-start | bytes 786440 | tf_op jit(solution)/shard_map/ppermute | solution.py:16
  252.3 19.8 %copy-start.10 = (f32[131072]{0:T(1024)}, f32[131072]{0:T(1024)S(1)}, u32[]{:S(2)}) copy-start(f32[131072]{0:T(1024)S(1)} %fusion.307) | copy-start | bytes 1572868
  252.4 11.5 %collective-permute-start.10 = (f32[4,128,128]{2,1,0:T(8,128)S(1)}, f32[4,128,128]{2,1,0:T(8,128)S(1)}, u32[]{:S(2)}, u32[]{:S(2)}) collective-permute-start(f32[4,128,128]{2,1,0:T(8,128)S(1)} %bitcast.198), channel_id=1, source_target_pairs={{1,0},{2,1},{3,2},{4,3},{5,4},{6,5},{7,6},{8,7},{9,8},{10,9},{11,1... | collective-permute-start | bytes 786440 | tf_op jit(solution)/shard_map/ppermute | solution.py:17
  254.3 15.1 %collective-permute-start.11 = (f32[4,128,128]{2,1,0:T(8,128)S(1)}, f32[4,128,128]{2,1,0:T(8,128)S(1)}, u32[]{:S(2)}, u32[]{:S(2)}) collective-permute-start(f32[4,128,128]{2,1,0:T(8,128)S(1)} %bitcast.197), channel_id=1, source_target_pairs={{0,1},{1,2},{2,3},{3,4},{4,5},{5,6},{6,7},{7,8},{8,9},{9,10},{10,1... | collective-permute-start | bytes 786440 | tf_op jit(solution)/shard_map/ppermute | solution.py:16
  289.8 18.0 %collective-permute-start.12 = (f32[4,128,128]{2,1,0:T(8,128)}, f32[4,128,128]{2,1,0:T(8,128)}, u32[]{:S(2)}, u32[]{:S(2)}) collective-permute-start(f32[4,128,128]{2,1,0:T(8,128)} %bitcast.42), channel_id=1, source_target_pairs={{1,0},{2,1},{3,2},{4,3},{5,4},{6,5},{7,6},{8,7},{9,8},{10,9},{11,1... | collective-permute-start | bytes 786440 | tf_op jit(solution)/shard_map/ppermute | solution.py:17
  291.7 16.5 %collective-permute-start.13 = (f32[4,128,128]{2,1,0:T(8,128)}, f32[4,128,128]{2,1,0:T(8,128)}, u32[]{:S(2)}, u32[]{:S(2)}) collective-permute-start(f32[4,128,128]{2,1,0:T(8,128)} %bitcast.43), channel_id=1, source_target_pairs={{0,1},{1,2},{2,3},{3,4},{4,5},{5,6},{6,7},{7,8},{8,9},{9,10},{10,1... | collective-permute-start | bytes 786440 | tf_op jit(solution)/shard_map/ppermute | solution.py:16
  323.6 133.3 %collective-permute-start.14 = (f32[4,128,128]{2,1,0:T(8,128)S(1)}, f32[4,128,128]{2,1,0:T(8,128)S(1)}, u32[]{:S(2)}, u32[]{:S(2)}) collective-permute-start(f32[4,128,128]{2,1,0:T(8,128)S(1)} %get-tuple-element.55), channel_id=1, source_target_pairs={{1,0},{2,1},{3,2},{4,3},{5,4},{6,5},{7,6},{8,7},{9,8},{10,9},{11,1... | collective-permute-start | bytes 786440 | tf_op jit(solution)/shard_map/ppermute | solution.py:17
  325.5 13.0 %copy-start.39 = (u32[256]{0:T(256)S(1)}, u32[256]{0:T(256)}, u32[]{:S(2)}) copy-start(u32[256]{0:T(256)} %constant.194) | copy-start | bytes 3076
  325.5 131.4 %collective-permute-start.15 = (f32[4,128,128]{2,1,0:T(8,128)S(1)}, f32[4,128,128]{2,1,0:T(8,128)}, u32[]{:S(2)}, u32[]{:S(2)}) collective-permute-start(f32[4,128,128]{2,1,0:T(8,128)S(1)} %get-tuple-element.56), channel_id=1, source_target_pairs={{0,1},{1,2},{2,3},{3,4},{4,5},{5,6},{6,7},{7,8},{8,9},{9,10},{10,1... | collective-permute-start | bytes 786440 | tf_op jit(solution)/shard_map/ppermute | solution.py:16
  338.1 120.6 %copy-start.1 = (f32[131072]{0:T(1024)S(1)}, f32[131072]{0:T(1024)}, u32[]{:S(2)}) copy-start(f32[131072]{0:T(1024)} %scatter_fusion.2) | copy-start | bytes 1572868
  338.2 183.1 %reduce-scatter.2.cloned.1.call-start = ((), (), s32[]{:S(2)}) async-start(), calls=%async_computation.2 | async-start | bytes 557056 | tf_op jit(solution)/shard_map/reduce_scatter | solution.py:151
  (27 other events, 153.7 us)
Sparse Core Ops, SparseCore 0:
  338.3 117.3 all-reduce.10
  458.8 62.5 reduce-scatter.1
where the time goes:
time: 530 us; the launch traced here: 528 us
  waiting for transfers between devices  271 us (51%)
  other arithmetic  105 us (20%)
  starting transfers between devices  78.5 us (15%)
  local copies, waits for them, and re-layouts  56.5 us (11%)
  between operations  16.6 us (3%)
    unnamed x3, waiting for transfers between devices  116 us
    ppermute x8, waiting for transfers between devices, padded_2(): after = lax.ppermute(initial, axis, down)  87.5 us
    ppermute x8, starting transfers between devices, padded_2(): before = lax.ppermute(last, axis, up)  51 us
    reduce_scatter x1, waiting for transfers between devices, body(): lax.psum_scatter(partial_value, 'shot', scatter_dimension=1, tiled=True)  50.8 us
    add x4, other arithmetic, advance(): 2.0 * current_ext[4:-4] - before + courant * laplace(current_ext)  32.8 us
    scatter-add x8, other arithmetic, inject(): flattened = field.reshape(-1).at[target].add(values, mode='drop')  28.2 us
    ppermute x8, waiting for transfers between devices, padded_2(): before = lax.ppermute(last, axis, up)  17.1 us
    add x4, other arithmetic, retreat(): earlier = 2.0 * current - following + laplace(weighted_ext)  16.5 us
  transfers between devices with their start and end apart: 19, of which 10 were waited for; matrix products, arithmetic and copies ran while one was open for 14% of the time, Pallas kernels for 0%

commit v1 on v0

--- a/solution.py
+++ b/solution.py
@@ -4,6 +4,15 @@
 from jax.sharding import PartitionSpec as P
 
 STENCIL = (-205.0 / 72.0, 8.0 / 5.0, -1.0 / 5.0, 8.0 / 315.0, -1.0 / 560.0)
+return_all_the_circles = lambda a0, lane_axis: jnp.concatenate(
+    lax.all_to_all(
+        jnp.stack(jnp.split(a0, lax.axis_size(lane_axis), 1), 0),
+        split_axis=0,
+        axis_name=lane_axis,
+        concat_axis=0,
+    ),
+    1,
+)
 
 
 def padded_2(array, sides, width):
@@ -100,7 +109,7 @@
         .set(payload)
     )
     outgoing = outgoing.reshape(2, devices, capacity, block_rows, breadth)
-    incoming = lax.all_to_all(outgoing, "space", split_axis=1, concat_axis=1, tiled=True)
+    incoming = return_all_the_circles(outgoing, "space")
     incoming = incoming.reshape(2, devices * capacity, block_rows, breadth)
     sender_grid = jnp.arange(devices, dtype=jnp.int32)[:, None] * capacity + ranking
     owned = peer_grid == position

time: 530 us -> 545 us (1.028)
  local copies, waits for them, and re-layouts: 56.5 us -> 71.1 us
    unnamed x81 -> x98, local copies, waits for them, and re-layouts: 3.47 us -> 22.1 us
  transfers between devices with their start and end apart: 19 -> 19, of which waited for: 10 -> 9; matrix products, arithmetic and copies ran while one was open for 14% -> 13% of each run, Pallas kernels for 0% -> 0%
where the time goes in v1:
time: 545 us; the launch traced here: 543 us
  waiting for transfers between devices  271 us (50%)
  other arithmetic  106 us (19%)
  starting transfers between devices  78.5 us (14%)
  local copies, waits for them, and re-layouts  71.1 us (13%)
  between operations  16.7 us (3%)
    unnamed x3, waiting for transfers between devices  116 us
    ppermute x8, waiting for transfers between devices, padded_2(): after = lax.ppermute(initial, axis, down)  87.3 us
    ppermute x8, starting transfers between devices, padded_2(): before = lax.ppermute(last, axis, up)  51 us
    reduce_scatter x1, waiting for transfers between devices, body(): lax.psum_scatter(partial_value, 'shot', scatter_dimension=1, tiled=True)  50.9 us
    add x4, other arithmetic, advance(): 2.0 * current_ext[4:-4] - before + courant * laplace(current_ext)  33 us
    scatter-add x8, other arithmetic, inject(): flattened = field.reshape(-1).at[target].add(values, mode='drop')  28.2 us
    unnamed x98, local copies, waits for them, and re-layouts  22.1 us
    add x4, other arithmetic, retreat(): earlier = 2.0 * current - following + laplace(weighted_ext)  16.9 us
  transfers between devices with their start and end apart: 19, of which 9 were waited for; matrix products, arithmetic and copies ran while one was open for 13% of the time, Pallas kernels for 0%

profile of v1, /device:TPU:4, one launch (start us, length us, event | category | flops | bytes accessed | tf_op | source)
XLA Modules:
  0.0 543.2 jit_solution(3577778192889454916)
XLA Ops:
  14.6 13.6 %scatter_fusion.3 = f32[2,512,8,128]{3,2,1,0:T(8,128)} fusion(f32[2,512,8,128]{3,2,1,0:T(8,128)} %broadcast_in_dim.48, s32[128]{0:T(128)S(1)} %fusion.326, f32[128,2,8,128]{3,2,1,0:T(8,128)S(1)} %copy.95), kind=kCustom, calls=%fused_computation.6 | custom fusion | bytes 3146240 | tf_op jit(solution)/shard_map/scatter | solution.py:109
  47.5 11.6 %all-to-all-start = ((f32[16,2,1,32,8,128]{5,4,3,1,2,0:T(8,128)}), f32[16,2,1,32,8,128]{5,4,3,1,2,0:T(8,128)}, u32[]{:S(2)}, u32[]{:S(2)}) async-start(f32[16,2,1,32,8,128]{5,4,3,1,2,0:T(8,128)} %fusion.304), calls=%async_computation | async-start | bytes 8388608 | tf_op jit(solution)/shard_map/all_to_all | solution.py:8
  61.4 6.2 %collective-permute-start.1 = (f32[4,128,128]{2,1,0:T(8,128)S(1)}, f32[4,128,128]{2,1,0:T(8,128)S(1)}, u32[]{:S(2)}, u32[]{:S(2)}) collective-permute-start(f32[4,128,128]{2,1,0:T(8,128)S(1)} %get-tuple-element.64), channel_id=1, source_target_pairs={{0,1},{1,2},{2,3},{3,4},{4,5},{5,6},{6,7},{7,8},{8,9},{9,10},{10,1... | collective-permute-start | bytes 786440 | tf_op jit(solution)/shard_map/ppermute | solution.py:25
  67.8 8.0 %scatter_custom_fusion.3 = s32[128]{0:T(128)S(1)} fusion(s32[2048]{0:T(1024)S(1)} %bitcast.323, s32[2048]{0:T(1024)S(1)} %add_bitcast_fusion, s32[]{:T(128)} %constant.152.clone.1), kind=kCustom, calls=%fused_computation.596 | custom fusion | bytes 516 | tf_op jit(solution)/shard_map/scatter | solution.py:120
  78.3 82.4 %collective-permute-done = f32[4,128,128]{2,1,0:T(8,128)S(1)} collective-permute-done((f32[4,128,128]{2,1,0:T(8,128)S(1)}, f32[4,128,128]{2,1,0:T(8,128)S(1)}, u32[]{:S(2)}, u32[]{:S(2)}) %collective-permute-start) | collective-permute-done | bytes 262176 | tf_op jit(solution)/shard_map/ppermute | solution.py:26
  163.2 3.5 fusion.199
  166.7 3.7 scatter_fusion
  172.6 6.3 %collective-permute-start.3 = (f32[4,128,128]{2,1,0:T(8,128)S(1)}, f32[4,128,128]{2,1,0:T(8,128)}, u32[]{:S(2)}, u32[]{:S(2)}) collective-permute-start(f32[4,128,128]{2,1,0:T(8,128)S(1)} %get-tuple-element.62), channel_id=1, source_target_pairs={{0,1},{1,2},{2,3},{3,4},{4,5},{5,6},{6,7},{7,8},{8,9},{9,10},{10,1... | collective-permute-start | bytes 786440 | tf_op jit(solution)/shard_map/ppermute | solution.py:25
  182.4 5.6 %collective-permute-done.3 = f32[4,128,128]{2,1,0:T(8,128)} collective-permute-done((f32[4,128,128]{2,1,0:T(8,128)S(1)}, f32[4,128,128]{2,1,0:T(8,128)}, u32[]{:S(2)}, u32[]{:S(2)}) %collective-permute-start.3) | collective-permute-done | bytes 262176 | tf_op jit(solution)/shard_map/ppermute | solution.py:25
  189.8 4.7 copy.112
  194.4 4.0 gather_fusion
  201.8 6.6 %collective-permute-start.7 = (f32[4,128,128]{2,1,0:T(8,128)S(1)}, f32[4,128,128]{2,1,0:T(8,128)S(1)}, u32[]{:S(2)}, u32[]{:S(2)}) collective-permute-start(f32[4,128,128]{2,1,0:T(8,128)S(1)} %bitcast.312), channel_id=1, source_target_pairs={{0,1},{1,2},{2,3},{3,4},{4,5},{5,6},{6,7},{7,8},{8,9},{9,10},{10,1... | collective-permute-start | bytes 786440 | tf_op jit(solution)/shard_map/ppermute | solution.py:25
  212.5 5.5 %collective-permute-done.7 = f32[4,128,128]{2,1,0:T(8,128)S(1)} collective-permute-done((f32[4,128,128]{2,1,0:T(8,128)S(1)}, f32[4,128,128]{2,1,0:T(8,128)S(1)}, u32[]{:S(2)}, u32[]{:S(2)}) %collective-permute-start.7) | collective-permute-done | bytes 262176 | tf_op jit(solution)/shard_map/ppermute | solution.py:25
  220.1 11.8 %fusion.124 = f32[8,128,128]{2,1,0:T(8,128)S(1)} fusion(f32[8,128,128]{2,1,0:T(8,128)S(1)} %copy-done.3, f32[8,128,128]{2,1,0:T(8,128)S(1)} %bitcast.301, f32[4,128,128]{2,1,0:T(8,128)} %copy-done.32, f32[4,128,128]{2,1,0:T(8,128)} %copy-done.31, f32[16,136,136]{2,1,0:T(8,128)} %select_maximum_fusion.8, f32[8,128,128]{2,1,0:T(8,128)} %bitcast.307), kind=kLoop, calls=%fused_computation.252 | loop fusion | flops 6422528 | bytes 11010048 | tf_op jit(solution)/shard_map/add | solution.py:65
  236.7 6.3 %collective-permute-start.9 = (f32[4,128,128]{2,1,0:T(8,128)}, f32[4,128,128]{2,1,0:T(8,128)}, u32[]{:S(2)}, u32[]{:S(2)}) collective-permute-start(f32[4,128,128]{2,1,0:T(8,128)} %bitcast.50), channel_id=1, source_target_pairs={{0,1},{1,2},{2,3},{3,4},{4,5},{5,6},{6,7},{7,8},{8,9},{9,10},{10,1... | collective-permute-start | bytes 786440 | tf_op jit(solution)/shard_map/ppermute | solution.py:25
  246.5 3.8 scatter_fusion.1
  253.2 6.3 %collective-permute-start.5 = (f32[4,128,128]{2,1,0:T(8,128)}, f32[4,128,128]{2,1,0:T(8,128)}, u32[]{:S(2)}, u32[]{:S(2)}) collective-permute-start(f32[4,128,128]{2,1,0:T(8,128)} %get-tuple-element.60), channel_id=1, source_target_pairs={{0,1},{1,2},{2,3},{3,4},{4,5},{5,6},{6,7},{7,8},{8,9},{9,10},{10,1... | collective-permute-start | bytes 786440 | tf_op jit(solution)/shard_map/ppermute | solution.py:25
  261.2 3.5 fusion.98
  268.9 6.5 %collective-permute-start.11 = (f32[4,128,128]{2,1,0:T(8,128)S(1)}, f32[4,128,128]{2,1,0:T(8,128)S(1)}, u32[]{:S(2)}, u32[]{:S(2)}) collective-permute-start(f32[4,128,128]{2,1,0:T(8,128)S(1)} %bitcast.310), channel_id=1, source_target_pairs={{0,1},{1,2},{2,3},{3,4},{4,5},{5,6},{6,7},{7,8},{8,9},{9,10},{10,1... | collective-permute-start | bytes 786440 | tf_op jit(solution)/shard_map/ppermute | solution.py:25
  278.4 5.5 %collective-permute-done.11 = f32[4,128,128]{2,1,0:T(8,128)S(1)} collective-permute-done((f32[4,128,128]{2,1,0:T(8,128)S(1)}, f32[4,128,128]{2,1,0:T(8,128)S(1)}, u32[]{:S(2)}, u32[]{:S(2)}) %collective-permute-start.11) | collective-permute-done | bytes 262176 | tf_op jit(solution)/shard_map/ppermute | solution.py:25
  286.7 12.5 %fusion.72 = f32[8,128,128]{2,1,0:T(8,128)} fusion(f32[8,128,128]{2,1,0:T(8,128)S(1)} %copy-done.5, f32[8,128,128]{2,1,0:T(8,128)S(1)} %bitcast.275, f32[4,128,128]{2,1,0:T(8,128)} %copy-done.30, f32[4,128,128]{2,1,0:T(8,128)} %copy-done.29, f32[16,136,136]{2,1,0:T(8,128)} %select_maximum_fusion.4, f32[8,128,128]{2,1,0:T(8,128)S(1)} %bitcast.271), kind=kLoop, calls=%fused_computation.200 | loop fusion | flops 6422528 | bytes 11010048 | tf_op jit(solution)/shard_map/add | solution.py:65
  299.2 3.4 fusion.324
  306.4 6.3 %collective-permute-start.13 = (f32[4,128,128]{2,1,0:T(8,128)}, f32[4,128,128]{2,1,0:T(8,128)}, u32[]{:S(2)}, u32[]{:S(2)}) collective-permute-start(f32[4,128,128]{2,1,0:T(8,128)} %bitcast.60), channel_id=1, source_target_pairs={{0,1},{1,2},{2,3},{3,4},{4,5},{5,6},{6,7},{7,8},{8,9},{9,10},{10,1... | collective-permute-start | bytes 786440 | tf_op jit(solution)/shard_map/ppermute | solution.py:25
  312.8 5.2 fusion.149
  317.9 5.0 scatter_fusion.2
  324.9 5.0 fusion.46
  340.4 6.3 %collective-permute-start.15 = (f32[4,128,128]{2,1,0:T(8,128)S(1)}, f32[4,128,128]{2,1,0:T(8,128)}, u32[]{:S(2)}, u32[]{:S(2)}) collective-permute-start(f32[4,128,128]{2,1,0:T(8,128)S(1)} %get-tuple-element.56), channel_id=1, source_target_pairs={{0,1},{1,2},{2,3},{3,4},{4,5},{5,6},{6,7},{7,8},{8,9},{9,10},{10,1... | collective-permute-start | bytes 786440 | tf_op jit(solution)/shard_map/ppermute | solution.py:25
  346.7 5.5 %gather_fusion.1 = f32[2048,128]{1,0:T(8,128)S(1)} fusion(f32[1024,128]{1,0:T(8,128)S(1)} %fusion.293, s32[2048]{0:T(1024)S(1)} %broadcast_clamp_fusion), kind=kCustom, calls=%fused_computation.1 | custom fusion | bytes 2105344 | tf_op jit(solution)/shard_map/gather | solution.py:159
  354.6 116.2 %all-reduce.11.cloned.1.call-done = f32[128,128]{1,0:T(8,128)} async-done(((f32[128,128]{1,0:T(8,128)}), f32[128,128]{1,0:T(8,128)}) %all-reduce.11.cloned.1.call-update) | async-done | bytes 65552
  473.8 4.8 fusion.20
  478.6 4.8 scatter_fusion.4
  485.5 50.9 %reduce-scatter.2.cloned.1.call-done = f32[8,8,128]{2,1,0:T(8,128)} async-done(((f32[8,128,128]{2,1,0:T(8,128)}), f32[8,8,128]{2,1,0:T(8,128)}) %reduce-scatter.2.cloned.1.call-update) | async-done | bytes 32784 | tf_op jit(solution)/shard_map/reduce_scatter | solution.py:160
  (176 shorter events, 94.9 us)
Async XLA Ops:
  28.2 13.5 %copy-start.12 = (f32[2,512,8,128]{3,2,1,0:T(8,128)S(1)}, f32[2,512,8,128]{3,2,1,0:T(8,128)}, u32[]{:S(2)}) copy-start(f32[2,512,8,128]{3,2,1,0:T(8,128)} %scatter_fusion.3) | copy-start | bytes 12582916
  47.5 142.3 %all-to-all-start = ((f32[16,2,1,32,8,128]{5,4,3,1,2,0:T(8,128)}), f32[16,2,1,32,8,128]{5,4,3,1,2,0:T(8,128)}, u32[]{:S(2)}, u32[]{:S(2)}) async-start(f32[16,2,1,32,8,128]{5,4,3,1,2,0:T(8,128)} %fusion.304), calls=%async_computation | async-start | bytes 8388608 | tf_op jit(solution)/shard_map/all_to_all | solution.py:8
  59.1 17.9 %copy-start.37 = (s32[1,512]{1,0:T(1,128)S(1)}, s32[1,512]{1,0:T(1,128)}, u32[]{:S(2)}) copy-start(s32[1,512]{1,0:T(1,128)} %param.23) | copy-start | bytes 6148
  59.1 17.9 %copy-start.34 = (f32[1,4,512]{2,1,0:T(4,128)S(1)}, f32[1,4,512]{2,1,0:T(4,128)}, u32[]{:S(2)}) copy-start(f32[1,4,512]{2,1,0:T(4,128)} %param.24) | copy-start | bytes 24580
  59.1 18.5 %copy-start.36 = (f32[1,4]{1,0:T(1,128)S(1)}, f32[1,4]{1,0:T(1,128)}, u32[]{:S(2)}) copy-start(f32[1,4]{1,0:T(1,128)} %param.21) | copy-start | bytes 52
  59.1 19.2 %copy-start.35 = (s32[1,128,16]{1,2,0:T(8,128)S(1)}, s32[1,128,16]{1,2,0:T(8,128)}, u32[]{:S(2)}) copy-start(s32[1,128,16]{1,2,0:T(8,128)} %param.25) | copy-start | bytes 24580
  59.1 411.6 %all-reduce.11.cloned.1.call-start = ((), (), s32[]{:S(2)}) async-start(), calls=%async_computation.3 | async-start | bytes 131072
  59.3 101.4 %copy-start.23 = (f32[8,128,128]{2,1,0:T(8,128)}, f32[8,128,128]{2,1,0:T(8,128)S(1)}, u32[]{:S(2)}) copy-start(f32[8,128,128]{2,1,0:T(8,128)S(1)} %bitcast_multiply_fusion.5) | copy-start | bytes 1572868
  59.3 101.4 %collective-permute-start = (f32[4,128,128]{2,1,0:T(8,128)S(1)}, f32[4,128,128]{2,1,0:T(8,128)S(1)}, u32[]{:S(2)}, u32[]{:S(2)}) collective-permute-start(f32[4,128,128]{2,1,0:T(8,128)S(1)} %get-tuple-element.63), channel_id=1, source_target_pairs={{1,0},{2,1},{3,2},{4,3},{5,4},{6,5},{7,6},{8,7},{9,8},{10,9},{11,1... | collective-permute-start | bytes 786440 | tf_op jit(solution)/shard_map/ppermute | solution.py:26
  61.4 99.3 %collective-permute-start.1 = (f32[4,128,128]{2,1,0:T(8,128)S(1)}, f32[4,128,128]{2,1,0:T(8,128)S(1)}, u32[]{:S(2)}, u32[]{:S(2)}) collective-permute-start(f32[4,128,128]{2,1,0:T(8,128)S(1)} %get-tuple-element.64), channel_id=1, source_target_pairs={{0,1},{1,2},{2,3},{3,4},{4,5},{5,6},{6,7},{7,8},{8,9},{9,10},{10,1... | collective-permute-start | bytes 786440 | tf_op jit(solution)/shard_map/ppermute | solution.py:25
  170.6 11.8 %collective-permute-start.2 = (f32[4,128,128]{2,1,0:T(8,128)S(1)}, f32[4,128,128]{2,1,0:T(8,128)S(1)}, u32[]{:S(2)}, u32[]{:S(2)}) collective-permute-start(f32[4,128,128]{2,1,0:T(8,128)S(1)} %get-tuple-element.61), channel_id=1, source_target_pairs={{1,0},{2,1},{3,2},{4,3},{5,4},{6,5},{7,6},{8,7},{9,8},{10,9},{11,1... | collective-permute-start | bytes 786440 | tf_op jit(solution)/shard_map/ppermute | solution.py:26
  172.6 15.4 %collective-permute-start.3 = (f32[4,128,128]{2,1,0:T(8,128)S(1)}, f32[4,128,128]{2,1,0:T(8,128)}, u32[]{:S(2)}, u32[]{:S(2)}) collective-permute-start(f32[4,128,128]{2,1,0:T(8,128)S(1)} %get-tuple-element.62), channel_id=1, source_target_pairs={{0,1},{1,2},{2,3},{3,4},{4,5},{5,6},{6,7},{7,8},{8,9},{9,10},{10,1... | collective-permute-start | bytes 786440 | tf_op jit(solution)/shard_map/ppermute | solution.py:25
  199.9 12.6 %collective-permute-start.6 = (f32[4,128,128]{2,1,0:T(8,128)S(1)}, f32[4,128,128]{2,1,0:T(8,128)S(1)}, u32[]{:S(2)}, u32[]{:S(2)}) collective-permute-start(f32[4,128,128]{2,1,0:T(8,128)S(1)} %bitcast.313), channel_id=1, source_target_pairs={{1,0},{2,1},{3,2},{4,3},{5,4},{6,5},{7,6},{8,7},{9,8},{10,9},{11,1... | collective-permute-start | bytes 786440 | tf_op jit(solution)/shard_map/ppermute | solution.py:26
  201.8 18.2 %copy-start.3 = (f32[8,128,128]{2,1,0:T(8,128)S(1)}, f32[8,128,128]{2,1,0:T(8,128)}, u32[]{:S(2)}) copy-start(f32[8,128,128]{2,1,0:T(8,128)} %param.17) | copy-start | bytes 1572868
  201.8 16.2 %collective-permute-start.7 = (f32[4,128,128]{2,1,0:T(8,128)S(1)}, f32[4,128,128]{2,1,0:T(8,128)S(1)}, u32[]{:S(2)}, u32[]{:S(2)}) collective-permute-start(f32[4,128,128]{2,1,0:T(8,128)S(1)} %bitcast.312), channel_id=1, source_target_pairs={{0,1},{1,2},{2,3},{3,4},{4,5},{5,6},{6,7},{7,8},{8,9},{9,10},{10,1... | collective-permute-start | bytes 786440 | tf_op jit(solution)/shard_map/ppermute | solution.py:25
  209.4 22.6 %copy-start.14 = (f32[1,128,8,128]{3,2,0,1:T(8,128)}, f32[1,128,8,128]{3,2,0,1:T(8,128)S(1)}, u32[]{:S(2)}) copy-start(f32[1,128,8,128]{3,2,0,1:T(8,128)S(1)} %get-tuple-element.52) | copy-start | bytes 1572868
  220.1 23.0 %copy-start.21 = (f32[8,128,128]{2,1,0:T(8,128)S(1)}, f32[8,128,128]{2,1,0:T(8,128)}, u32[]{:S(2)}) copy-start(f32[8,128,128]{2,1,0:T(8,128)} %copy-done.20) | copy-start | bytes 1572868
  233.9 12.6 %copy-start.7 = (f32[131072]{0:T(1024)}, f32[131072]{0:T(1024)S(1)}, u32[]{:S(2)}) copy-start(f32[131072]{0:T(1024)S(1)} %fusion.322) | copy-start | bytes 1572868
  234.8 24.7 %collective-permute-start.8 = (f32[4,128,128]{2,1,0:T(8,128)}, f32[4,128,128]{2,1,0:T(8,128)}, u32[]{:S(2)}, u32[]{:S(2)}) collective-permute-start(f32[4,128,128]{2,1,0:T(8,128)} %bitcast.49), channel_id=1, source_target_pairs={{1,0},{2,1},{3,2},{4,3},{5,4},{6,5},{7,6},{8,7},{9,8},{10,9},{11,1... | collective-permute-start | bytes 786440 | tf_op jit(solution)/shard_map/ppermute | solution.py:26
  236.7 22.8 %collective-permute-start.9 = (f32[4,128,128]{2,1,0:T(8,128)}, f32[4,128,128]{2,1,0:T(8,128)}, u32[]{:S(2)}, u32[]{:S(2)}) collective-permute-start(f32[4,128,128]{2,1,0:T(8,128)} %bitcast.50), channel_id=1, source_target_pairs={{0,1},{1,2},{2,3},{3,4},{4,5},{5,6},{6,7},{7,8},{8,9},{9,10},{10,1... | collective-permute-start | bytes 786440 | tf_op jit(solution)/shard_map/ppermute | solution.py:25
  251.3 24.2 %collective-permute-start.4 = (f32[4,128,128]{2,1,0:T(8,128)}, f32[4,128,128]{2,1,0:T(8,128)S(1)}, u32[]{:S(2)}, u32[]{:S(2)}) collective-permute-start(f32[4,128,128]{2,1,0:T(8,128)} %get-tuple-element.59), channel_id=1, source_target_pairs={{1,0},{2,1},{3,2},{4,3},{5,4},{6,5},{7,6},{8,7},{9,8},{10,9},{11,1... | collective-permute-start | bytes 786440 | tf_op jit(solution)/shard_map/ppermute | solution.py:26
  253.2 22.3 %collective-permute-start.5 = (f32[4,128,128]{2,1,0:T(8,128)}, f32[4,128,128]{2,1,0:T(8,128)}, u32[]{:S(2)}, u32[]{:S(2)}) collective-permute-start(f32[4,128,128]{2,1,0:T(8,128)} %get-tuple-element.60), channel_id=1, source_target_pairs={{0,1},{1,2},{2,3},{3,4},{4,5},{5,6},{6,7},{7,8},{8,9},{9,10},{10,1... | collective-permute-start | bytes 786440 | tf_op jit(solution)/shard_map/ppermute | solution.py:25
  266.9 19.8 %copy-start.10 = (f32[131072]{0:T(1024)}, f32[131072]{0:T(1024)S(1)}, u32[]{:S(2)}) copy-start(f32[131072]{0:T(1024)S(1)} %fusion.323) | copy-start | bytes 1572868
  266.9 11.5 %collective-permute-start.10 = (f32[4,128,128]{2,1,0:T(8,128)S(1)}, f32[4,128,128]{2,1,0:T(8,128)S(1)}, u32[]{:S(2)}, u32[]{:S(2)}) collective-permute-start(f32[4,128,128]{2,1,0:T(8,128)S(1)} %bitcast.311), channel_id=1, source_target_pairs={{1,0},{2,1},{3,2},{4,3},{5,4},{6,5},{7,6},{8,7},{9,8},{10,9},{11,1... | collective-permute-start | bytes 786440 | tf_op jit(solution)/shard_map/ppermute | solution.py:26
  268.9 15.1 %collective-permute-start.11 = (f32[4,128,128]{2,1,0:T(8,128)S(1)}, f32[4,128,128]{2,1,0:T(8,128)S(1)}, u32[]{:S(2)}, u32[]{:S(2)}) collective-permute-start(f32[4,128,128]{2,1,0:T(8,128)S(1)} %bitcast.310), channel_id=1, source_target_pairs={{0,1},{1,2},{2,3},{3,4},{4,5},{5,6},{6,7},{7,8},{8,9},{9,10},{10,1... | collective-permute-start | bytes 786440 | tf_op jit(solution)/shard_map/ppermute | solution.py:25
  304.5 18.4 %collective-permute-start.12 = (f32[4,128,128]{2,1,0:T(8,128)}, f32[4,128,128]{2,1,0:T(8,128)}, u32[]{:S(2)}, u32[]{:S(2)}) collective-permute-start(f32[4,128,128]{2,1,0:T(8,128)} %bitcast.59), channel_id=1, source_target_pairs={{1,0},{2,1},{3,2},{4,3},{5,4},{6,5},{7,6},{8,7},{9,8},{10,9},{11,1... | collective-permute-start | bytes 786440 | tf_op jit(solution)/shard_map/ppermute | solution.py:26
  306.4 16.5 %collective-permute-start.13 = (f32[4,128,128]{2,1,0:T(8,128)}, f32[4,128,128]{2,1,0:T(8,128)}, u32[]{:S(2)}, u32[]{:S(2)}) collective-permute-start(f32[4,128,128]{2,1,0:T(8,128)} %bitcast.60), channel_id=1, source_target_pairs={{0,1},{1,2},{2,3},{3,4},{4,5},{5,6},{6,7},{7,8},{8,9},{9,10},{10,1... | collective-permute-start | bytes 786440 | tf_op jit(solution)/shard_map/ppermute | solution.py:25
  338.4 133.6 %collective-permute-start.14 = (f32[4,128,128]{2,1,0:T(8,128)S(1)}, f32[4,128,128]{2,1,0:T(8,128)S(1)}, u32[]{:S(2)}, u32[]{:S(2)}) collective-permute-start(f32[4,128,128]{2,1,0:T(8,128)S(1)} %get-tuple-element.55), channel_id=1, source_target_pairs={{1,0},{2,1},{3,2},{4,3},{5,4},{6,5},{7,6},{8,7},{9,8},{10,9},{11,1... | collective-permute-start | bytes 786440 | tf_op jit(solution)/shard_map/ppermute | solution.py:26
  340.3 12.9 %copy-start.40 = (u32[256]{0:T(256)S(1)}, u32[256]{0:T(256)}, u32[]{:S(2)}) copy-start(u32[256]{0:T(256)} %constant.194) | copy-start | bytes 3076
  340.4 131.7 %collective-permute-start.15 = (f32[4,128,128]{2,1,0:T(8,128)S(1)}, f32[4,128,128]{2,1,0:T(8,128)}, u32[]{:S(2)}, u32[]{:S(2)}) collective-permute-start(f32[4,128,128]{2,1,0:T(8,128)S(1)} %get-tuple-element.56), channel_id=1, source_target_pairs={{0,1},{1,2},{2,3},{3,4},{4,5},{5,6},{6,7},{7,8},{8,9},{9,10},{10,1... | collective-permute-start | bytes 786440 | tf_op jit(solution)/shard_map/ppermute | solution.py:25
  352.9 120.8 %copy-start.1 = (f32[131072]{0:T(1024)S(1)}, f32[131072]{0:T(1024)}, u32[]{:S(2)}) copy-start(f32[131072]{0:T(1024)} %scatter_fusion.2) | copy-start | bytes 1572868
  353.0 183.4 %reduce-scatter.2.cloned.1.call-start = ((), (), s32[]{:S(2)}) async-start(), calls=%async_computation.2 | async-start | bytes 557056 | tf_op jit(solution)/shard_map/reduce_scatter | solution.py:160
  (28 other events, 165.3 us)
Sparse Core Ops, SparseCore 0:
  353.1 117.6 all-reduce.10
  473.8 62.5 reduce-scatter.1
